TPU v7x, 32 devices: a whole 2x2x4 slice. The times are simulated.
32 devices in a mesh: axial: 8 (over y, x, core), radial: 4 (over z).
Axes of the slice: x: 2, y: 2, z: 4, core: 2. Of those that a mesh axis runs over, the one named last changes fastest.
Arguments:
- composition_deviations: float32 [38, 1024, 512], P(None, 'axial', 'radial'), may hold values from -6 to 6
- flow_speed_vector: float32 [2, 1024, 512], P(None, 'axial', 'radial'), may hold values from -1 to 1
- thermal_field: float32 [1024, 512], P('axial', 'radial'), may hold values from 0.4 to 4
- linearized_kinetics_operator: float32 [38, 38], replicated, may hold values from -0.5 to 0.5
- frozen_jacobian_inverse_addend: float32 [38, 38], replicated, may hold values from -0.25 to 0.25
- rigid_block_indicator: int32 [512, 4], P('axial', 'radial'), may hold values from 0 to 1, as said below
- molar_absorptivity_table: float32 [4, 38], replicated, may hold values from -1 to 1
- spokewise_sightline_length: float32 [512], P('radial'), may hold values from 0.3 to 3
- sightline_lengthwise_index: int32 [4, 32768], replicated, may hold values from 0 to 1023
- observed_absorbance_traces: float32 [4, 32768], P(None, ('axial', 'radial')), may hold values from -6 to 6
Outputs:
- species_out: float32 [38, 1024, 512], P(None, 'axial', 'radial')
- misfit: float32 [4, 32768], P(None, ('axial', 'radial'))
Inputs may be any that keep to these rules, and one draw needn't show every extreme that they name: `rigid_block_indicator`: in each radial column of tiles, the tiles of 2 cyclically consecutive axial devices are all stiff and every other axial device holds exactly 8 stiff tiles, so the column holds 176 stiff tiles.
All inputs are finite; a program needn't handle non-finite values.
Results may differ from a plain program's by a relative error of at most 0.0001.
Values sent between devices are 32-bit elements; how exact they have to be, the bound alone decides.
No kernel may reach another device: no remote copies, remote signals or barrier semaphores. Data moves between devices by JAX's collectives and lax.ppermute only.
A program may use at most 192 MiB of HBM per device.

v0:
```python
import math

import jax
import jax.numpy as jnp
from jax import lax
from jax.sharding import PartitionSpec as P

TILE_ROWS = 2
ITERS = 3


TIME_STEP = 0.4
CHEM_STEP = 0.5
ARRHENIUS_BARRIER = 1.0
WENO_EPS = 1e-06
HIGHEST = lax.Precision.HIGHEST


def edge_layers(shard, axis, dim, width):
    peers, length = (lax.axis_size(axis), shard.shape[dim])
    up = [(i, i + 1) for i in range(peers - 1)]
    down = [(j, i) for i, j in up]
    last = lax.slice_in_dim(shard, length - width, length, axis=dim)
    initial = lax.slice_in_dim(shard, 0, width, axis=dim)
    return lax.ppermute(last, axis, up), lax.ppermute(initial, axis, down)


def weno_side(minus_two, minus_one, centre, plus_one, plus_two):
    curve_zero = minus_two - 2.0 * minus_one + centre
    curve_one = minus_one - 2.0 * centre + plus_one
    curve_two = centre - 2.0 * plus_one + plus_two
    slope_zero = minus_two - 4.0 * minus_one + 3.0 * centre
    slope_one = minus_one - plus_one
    slope_two = 3.0 * centre - 4.0 * plus_one + plus_two
    beta_zero = 13.0 / 12.0 * curve_zero * curve_zero + 0.25 * slope_zero * slope_zero
    beta_one = 13.0 / 12.0 * curve_one * curve_one + 0.25 * slope_one * slope_one
    beta_two = 13.0 / 12.0 * curve_two * curve_two + 0.25 * slope_two * slope_two
    guard_zero = WENO_EPS + beta_zero
    guard_one = WENO_EPS + beta_one
    guard_two = WENO_EPS + beta_two
    guard_zero = guard_zero * guard_zero
    guard_one = guard_one * guard_one
    guard_two = guard_two * guard_two
    cross_zero = guard_one * guard_two
    cross_one = 6.0 * (guard_zero * guard_two)
    cross_two = 3.0 * (guard_zero * guard_one)
    blended = cross_zero * (2.0 * minus_two - 7.0 * minus_one + 11.0 * centre)
    blended = blended + cross_one * (-minus_one + 5.0 * centre + 2.0 * plus_one)
    blended = blended + cross_two * (2.0 * centre + 5.0 * plus_one - plus_two)
    return blended / (6.0 * (cross_zero + cross_one + cross_two))


def face_difference(field, speed, along, length):
    face_count = length + 1

    def cut_part(offset):
        return lax.slice_in_dim(field, offset, offset + face_count, axis=along)

    face_speed = 0.5 * (
        lax.slice_in_dim(speed, 2, 2 + face_count, axis=along)
        + lax.slice_in_dim(speed, 3, 3 + face_count, axis=along)
    )
    forward = face_speed >= 0.0
    stencil = [
        jnp.where(forward, cut_part(low), cut_part(high))
        for low, high in ((0, 5), (1, 4), (2, 3), (3, 2), (4, 1))
    ]
    face_flux = face_speed * weno_side(*stencil)
    return lax.slice_in_dim(face_flux, 1, face_count, axis=along) - lax.slice_in_dim(
        face_flux, 0, face_count - 1, axis=along
    )


def transport(species, speed, width=3):
    species_count = species.shape[0]
    along = []
    for component, (axis, dim) in enumerate((("axial", 1), ("radial", 2))):
        edges = jnp.concatenate([species, speed[component : component + 1]], axis=0)
        before, after = edge_layers(edges, axis, dim, width)
        field = jnp.concatenate([before[:species_count], species, after[:species_count]], axis=dim)
        velocity = jnp.concatenate(
            [before[species_count:], speed[component : component + 1], after[species_count:]],
            axis=dim,
        )
        along.append(face_difference(field, velocity, dim, species.shape[dim]))
    return species - TIME_STEP * (along[0] + along[1])


def kinetics_advance(
    starting_composition_field,
    thermal_field,
    linearized_kinetics_operator,
    frozen_jacobian_inverse_addend,
):
    acceleration_factor = jnp.exp(-ARRHENIUS_BARRIER / thermal_field)
    current = starting_composition_field
    for newton_step in range(ITERS):
        source = jnp.tensordot(
            linearized_kinetics_operator, current, axes=(1, 0), precision=HIGHEST
        ) - jnp.tanh(current)
        defect = current - starting_composition_field - CHEM_STEP * acceleration_factor * source
        current = (
            current
            - defect
            - jnp.tensordot(frozen_jacobian_inverse_addend, defect, axes=(1, 0), precision=HIGHEST)
        )
    return current


def absorbance_profile(field, molar_absorptivity_table, spokewise_sightline_length):
    mixed = jnp.tensordot(molar_absorptivity_table, field, axes=(1, 0), precision=HIGHEST)
    return jnp.dot(mixed, spokewise_sightline_length, precision=HIGHEST)


def butterfly_sum(part, axis):
    peers, stride = (lax.axis_size(axis), 1)
    if peers & (peers - 1):
        return lax.psum(part, axis)
    while stride < peers:
        pairs = [(j, j ^ stride) for j in range(peers)]
        part = part + lax.ppermute(part, axis, pairs)
        stride *= 2
    return part


def doubling_gather(part, axis):
    peers, stride = (lax.axis_size(axis), 1)
    if peers & (peers - 1):
        return lax.all_gather(part, axis, axis=1, tiled=True)
    position = lax.axis_index(axis)
    blocks = part[None]
    while stride < peers:
        pairs = [(j, j ^ stride) for j in range(peers)]
        other = lax.ppermute(blocks, axis, pairs)
        upper = (position // stride) % 2 == 1
        blocks = jnp.where(
            upper, jnp.concatenate([other, blocks], 0), jnp.concatenate([blocks, other], 0)
        )
        stride *= 2
    return jnp.transpose(blocks, (1, 0, 2)).reshape(part.shape[0], -1)


def gathered_profile(profile):
    return doubling_gather(butterfly_sum(profile, "radial"), "axial")


def local(
    composition_deviations,
    flow_speed_vector,
    thermal_field,
    linearized_kinetics_operator,
    frozen_jacobian_inverse_addend,
    rigid_block_indicator,
    molar_absorptivity_table,
    spokewise_sightline_length,
    sightline_lengthwise_index,
    observed_absorbance_traces,
):
    advected_composition_field = transport(composition_deviations, flow_speed_vector)
    combusted_composition_field = kinetics_advance(
        advected_composition_field,
        thermal_field,
        linearized_kinetics_operator,
        frozen_jacobian_inverse_addend,
    )
    flag_cells = jnp.repeat(
        jnp.repeat(rigid_block_indicator, TILE_ROWS, axis=0),
        advected_composition_field.shape[2],
        axis=1,
    )
    species_out = jnp.where(
        flag_cells[None] > 0, combusted_composition_field, advected_composition_field
    )
    path_scale = 1.0 / math.sqrt(advected_composition_field.shape[2] * lax.axis_size("radial"))
    profile = (
        absorbance_profile(species_out, molar_absorptivity_table, spokewise_sightline_length)
        * path_scale
    )
    whole_profile = gathered_profile(profile)
    device = lax.axis_index(("axial", "radial"))
    sample_count = observed_absorbance_traces.shape[1]
    own_rows = lax.dynamic_slice_in_dim(
        sightline_lengthwise_index, device * sample_count, sample_count, 1
    )
    cells = lax.broadcasted_iota(jnp.int32, (1, whole_profile.shape[1], 1), 1)
    values = jnp.sum(
        jnp.where(own_rows[:, None, :] == cells, whole_profile[:, :, None], 0.0), axis=1
    )
    return (species_out, values - observed_absorbance_traces)


def solution(mesh):
    in_specs = (
        P(None, "axial", "radial"),
        P(None, "axial", "radial"),
        P("axial", "radial"),
        P(),
        P(),
        P("axial", "radial"),
        P(),
        P("radial"),
        P(),
        P(None, ("axial", "radial")),
    )
    out_specs = (P(None, "axial", "radial"), P(None, ("axial", "radial")))
    return jax.shard_map(local, mesh=mesh, in_specs=in_specs, out_specs=out_specs, check_vma=False)
```

profile of v0, /device:TPU:0, one launch (start us, length us, event | category | flops | bytes accessed | tf_op | source)
XLA Modules:
  0.0 97.7 jit_solution(12041552857022919214)
XLA Ops:
  0.7 2.6 %copy.134 = f32[38,128,128]{1,0,2:T(8,128)S(1)} copy(f32[38,128,128]{2,1,0:T(8,128)} %param.10) | data formatting | bytes 4980736 | tf_op args[0]
  3.5 5.7 %collective-permute-start.2 = (f32[39,128,3]{1,0,2:T(8,128)S(1)}, f32[39,128,3]{1,0,2:T(8,128)}, u32[]{:S(2)}, u32[]{:S(2)}) collective-permute-start(f32[39,128,3]{1,0,2:T(8,128)S(1)} %get-tuple-element.18), channel_id=1, source_target_pairs={{0,1},{1,2},{2,3},{4,5},{5,6},{6,7},{8,9},{9,10},{10,11},{12,13},{... | collective-permute-start | bytes 179720 | tf_op jit(solution)/shard_map/ppermute | solution.py:25
  9.2 1.3 %collective-permute-start.3 = (f32[39,128,3]{1,0,2:T(8,128)S(1)}, f32[39,128,3]{1,0,2:T(8,128)}, u32[]{:S(2)}, u32[]{:S(2)}) collective-permute-start(f32[39,128,3]{1,0,2:T(8,128)S(1)} %get-tuple-element.19), channel_id=1, source_target_pairs={{1,0},{2,1},{3,2},{5,4},{6,5},{7,6},{9,8},{10,9},{11,10},{13,12},{... | collective-permute-start | bytes 179720 | tf_op jit(solution)/shard_map/ppermute | solution.py:25
  10.5 1.5 %copy.117 = f32[38,128,128]{2,0,1:T(8,128)S(1)} copy(f32[38,128,128]{2,1,0:T(8,128)S(1)} %copy-done.3) | data formatting | bytes 4980736 | tf_op args[0]
  12.6 2.1 %collective-permute-start = (f32[39,3,128]{2,0,1:T(8,128)}, f32[39,3,128]{2,0,1:T(8,128)}, u32[]{:S(2)}, u32[]{:S(2)}) collective-permute-start(f32[39,3,128]{2,0,1:T(8,128)} %get-tuple-element.16), channel_id=1, source_target_pairs={{0,4},{4,8},{8,12},{12,16},{16,20},{20,24},{24,28},{1,5},{5,9},{9,... | collective-permute-start | bytes 179720 | tf_op jit(solution)/shard_map/ppermute | solution.py:25
  14.7 1.3 %collective-permute-start.1 = (f32[39,3,128]{2,0,1:T(8,128)}, f32[39,3,128]{2,0,1:T(8,128)}, u32[]{:S(2)}, u32[]{:S(2)}) collective-permute-start(f32[39,3,128]{2,0,1:T(8,128)} %get-tuple-element.17), channel_id=1, source_target_pairs={{4,0},{8,4},{12,8},{16,12},{20,16},{24,20},{28,24},{5,1},{9,5},{13... | collective-permute-start | bytes 179720 | tf_op jit(solution)/shard_map/ppermute | solution.py:25
  16.4 0.7 slice.176
  17.1 0.7 slice.177
  17.8 0.7 slice.162
  20.1 3.1 %copy.123 = f32[38,3,128]{1,0,2:T(8,128)} copy(f32[38,3,128]{2,0,1:T(8,128)} %bitcast.92) | data formatting | bytes 116736 | tf_op jit(solution)/shard_map/slice | solution.py:80
  23.2 3.1 %copy.126 = f32[38,3,128]{1,0,2:T(8,128)} copy(f32[38,3,128]{2,0,1:T(8,128)} %bitcast.91) | data formatting | bytes 116736 | tf_op jit(solution)/shard_map/slice | solution.py:80
  26.3 9.6 %divide_multiply_fusion.1 = f32[38,128,129]{1,0,2:T(8,128)S(1)} fusion(f32[38,128,3]{1,0,2:T(8,128)} %bitcast.89, f32[38,128,128]{1,0,2:T(8,128)S(1)} %copy.134, f32[38,128,3]{1,0,2:T(8,128)} %bitcast.90, f32[128,129]{0,1:T(8,128)S(1)} %fusion.62, pred[128,129]{0,1:T(8,128)(4,1)S(1)} %compare_bitcast_fusion), kind=kLoop, calls=%fused_computation.61 | loop fusion | flops 47686656 | bytes 5199488 | tf_op jit(solution)/shard_map/mul | solution.py:68
  36.0 15.3 %divide_multiply_fusion = f32[38,129,128]{1,0,2:T(8,128)S(1)} fusion(f32[38,3,128]{1,0,2:T(8,128)S(1)} %copy-done.2, f32[38,128,128]{1,0,2:T(8,128)S(1)} %copy.134, f32[38,3,128]{1,0,2:T(8,128)S(1)} %copy-done.1, f32[129,128]{0,1:T(8,128)S(1)} %copy.121, pred[129,128]{0,1:T(8,128)(4,1)S(1)} %copy.122), kind=kLoop, calls=%fused_computation.32 | loop fusion | flops 47686656 | bytes 5199488 | tf_op jit(solution)/shard_map/mul | solution.py:68
  51.2 1.0 fusion.32
  52.2 2.3 %fusion.70 = f32[128,128,38]{0,2,1:T(8,128)S(1)} fusion(f32[38,128,128]{1,0,2:T(8,128)S(1)} %fusion.32, f32[38,38]{1,0:T(8,128)S(1)} %copy-done.4), kind=kOutput, calls=%fused_computation.117 | convolution fusion | flops 283901952 | bytes 4986512 | tf_op jit(solution)/shard_map/dot_general | solution.py:98
  54.6 4.0 %bitcast_subtract_fusion.4 = f32[38,128,128]{1,0,2:T(8,128)S(1)} fusion(f32[38,128,128]{1,0,2:T(8,128)S(1)} %fusion.32, f32[128,128,38]{0,2,1:T(8,128)S(1)} %fusion.70, f32[128,128]{0,1:T(8,128)S(1)} %copy.135, f32[38,38]{1,0:T(8,128)S(1)} %copy-done.6), kind=kOutput, calls=%fused_computation.78 | convolution fusion | flops 290127872 | bytes 7542416 | tf_op jit(solution)/shard_map/dot_general | solution.py:105
  58.6 2.4 %fusion.68 = f32[128,128,38]{0,2,1:T(8,128)S(1)} fusion(f32[38,128,128]{1,0,2:T(8,128)S(1)} %bitcast_subtract_fusion.4, f32[38,38]{1,0:T(8,128)S(1)} %copy-done.4), kind=kOutput, calls=%fused_computation.115 | convolution fusion | flops 283901952 | bytes 4986512 | tf_op jit(solution)/shard_map/dot_general | solution.py:98
  61.0 4.5 %bitcast_subtract_fusion.2 = f32[38,128,128]{1,0,2:T(8,128)S(1)} fusion(f32[38,128,128]{1,0,2:T(8,128)S(1)} %bitcast_subtract_fusion.4, f32[128,128,38]{0,2,1:T(8,128)S(1)} %fusion.68, f32[38,128,128]{1,0,2:T(8,128)S(1)} %fusion.32, f32[128,128]{0,1:T(8,128)S(1)} %copy.135, f32[38,38]{1,0:T(8,128)S(1)} %copy-done.6), kind=kOutput, calls=%fused_computation.74 | convolution fusion | flops 290127872 | bytes 10032784 | tf_op jit(solution)/shard_map/dot_general | solution.py:105
  65.6 2.4 %fusion.66 = f32[128,128,38]{0,2,1:T(8,128)S(1)} fusion(f32[38,128,128]{1,0,2:T(8,128)S(1)} %bitcast_subtract_fusion.2, f32[38,38]{1,0:T(8,128)S(1)} %copy-done.4), kind=kOutput, calls=%fused_computation.113 | convolution fusion | flops 283901952 | bytes 4986512 | tf_op jit(solution)/shard_map/dot_general | solution.py:98
  68.0 4.3 %fusion.33 = f32[38,128,128]{1,0,2:T(8,128)S(1)} fusion(f32[38,128,128]{1,0,2:T(8,128)S(1)} %fusion.32, f32[38,128,128]{1,0,2:T(8,128)S(1)} %bitcast_subtract_fusion.2, f32[128,128,38]{0,2,1:T(8,128)S(1)} %fusion.66, f32[128,128]{0,1:T(8,128)S(1)} %copy.135, pred[128]{0:T(512)(128)(4,1)S(1)} %gt.22, f32[38,38]{1,0:T(8,128)S(1)} %copy-done.6), kind=kOutput, calls=%fused_computation.70 | convolution fusion | flops 290750464 | bytes 10032912 | tf_op jit(solution)/shard_map/dot_general | solution.py:105
  72.4 1.7 %convolution_bitcast_fusion = f32[4,128,128]{1,0,2:T(4,128)S(1)} fusion(f32[38,128,128]{1,0,2:T(8,128)S(1)} %fusion.33, f32[4,38]{1,0:T(4,128)S(1)} %copy-done.9), kind=kOutput, calls=%fused_computation.90 | convolution fusion | flops 29884416 | bytes 2753120 | tf_op jit(solution)/shard_map/dot_general | solution.py:111
  74.3 2.7 %collective-permute-start.4 = (f32[4,128]{1,0:T(4,128)S(1)}, f32[4,128]{1,0:T(4,128)S(1)}, u32[]{:S(2)}, u32[]{:S(2)}) collective-permute-start(f32[4,128]{1,0:T(4,128)S(1)} %broadcast_multiply_fusion), channel_id=1, source_target_pairs={{0,1},{1,0},{2,3},{3,2},{4,5},{5,4},{6,7},{7,6},{8,9},{9,8},{10,11... | collective-permute-start | bytes 6152 | tf_op jit(solution)/shard_map/ppermute | solution.py:121
  77.0 1.6 %collective-permute-done.4 = f32[4,128]{1,0:T(4,128)S(1)} collective-permute-done((f32[4,128]{1,0:T(4,128)S(1)}, f32[4,128]{1,0:T(4,128)S(1)}, u32[]{:S(2)}, u32[]{:S(2)}) %collective-permute-start.4) | collective-permute-done | bytes 2080 | tf_op jit(solution)/shard_map/ppermute | solution.py:121
  78.6 2.6 %collective-permute-start.5 = (f32[4,128]{1,0:T(4,128)S(1)}, f32[4,128]{1,0:T(4,128)S(1)}, u32[]{:S(2)}, u32[]{:S(2)}) collective-permute-start(f32[4,128]{1,0:T(4,128)S(1)} %fusion.75), channel_id=1, source_target_pairs={{0,2},{1,3},{2,0},{3,1},{4,6},{5,7},{6,4},{7,5},{8,10},{9,11},{10,... | collective-permute-start | bytes 6152 | tf_op jit(solution)/shard_map/ppermute | solution.py:121
  81.2 1.9 %collective-permute-done.5 = f32[4,128]{1,0:T(4,128)S(1)} collective-permute-done((f32[4,128]{1,0:T(4,128)S(1)}, f32[4,128]{1,0:T(4,128)S(1)}, u32[]{:S(2)}, u32[]{:S(2)}) %collective-permute-start.5) | collective-permute-done | bytes 2080 | tf_op jit(solution)/shard_map/ppermute | solution.py:121
  83.1 0.9 collective-permute-start.6
  83.9 0.8 collective-permute-done.6
  84.7 2.7 %collective-permute-start.7 = (f32[2,4,128]{2,0,1:T(2,128)S(1)}, f32[2,4,128]{2,0,1:T(2,128)S(1)}, u32[]{:S(2)}, u32[]{:S(2)}) collective-permute-start(f32[2,4,128]{2,0,1:T(2,128)S(1)} %maximum_select_fusion.2), channel_id=1, source_target_pairs={{0,8},{4,12},{8,0},{12,4},{16,24},{20,28},{24,16},{28,20},{1,9},{5... | collective-permute-start | bytes 12296 | tf_op jit(solution)/shard_map/ppermute | solution.py:134
  87.5 1.6 %collective-permute-done.7 = f32[2,4,128]{2,0,1:T(2,128)S(1)} collective-permute-done((f32[2,4,128]{2,0,1:T(2,128)S(1)}, f32[2,4,128]{2,0,1:T(2,128)S(1)}, u32[]{:S(2)}, u32[]{:S(2)}) %collective-permute-start.7) | collective-permute-done | bytes 4128 | tf_op jit(solution)/shard_map/ppermute | solution.py:134
  89.1 3.0 %collective-permute-start.8 = (f32[4,4,128]{2,0,1:T(4,128)S(1)}, f32[4,4,128]{2,0,1:T(4,128)S(1)}, u32[]{:S(2)}, u32[]{:S(2)}) collective-permute-start(f32[4,4,128]{2,0,1:T(4,128)S(1)} %maximum_select_fusion.1), channel_id=1, source_target_pairs={{0,16},{4,20},{8,24},{12,28},{16,0},{20,4},{24,8},{28,12},{1,17},{... | collective-permute-start | bytes 24584 | tf_op jit(solution)/shard_map/ppermute | solution.py:134
  92.1 2.1 %copy.136 = f32[38,128,128]{2,1,0:T(8,128)} copy(f32[38,128,128]{1,0,2:T(8,128)S(1)} %fusion.33) | data formatting | bytes 4980736
  94.3 2.8 %select_reduce_fusion = f32[4,1024]{1,0:T(4,128)S(1)} fusion(f32[4,1024]{1,0:T(4,128)S(1)} %bitcast.95, s32[4,1024]{1,0:T(4,128)S(1)} %constant_dynamic-slice_fusion), kind=kLoop, calls=%fused_computation | loop fusion | flops 12578816 | bytes 49152 | tf_op jit(solution)/shard_map/reduce_sum | solution.py:186
  (59 shorter events, 3.7 us)
Async XLA Ops:
  0.6 91.5 %copy-start = (s32[4,32768]{1,0:T(4,128)S(1)}, s32[4,32768]{1,0:T(4,128)}, u32[]{:S(2)}) copy-start(s32[4,32768]{1,0:T(4,128)} %param.18) | copy-start | bytes 1572868
  0.6 2.7 %copy-start.5 = (f32[2,128,128]{2,1,0:T(8,128)S(1)}, f32[2,128,128]{2,1,0:T(8,128)}, u32[]{:S(2)}) copy-start(f32[2,128,128]{2,1,0:T(8,128)} %param.11) | copy-start | bytes 393220
  3.4 7.0 %copy-start.3 = (f32[38,128,128]{2,1,0:T(8,128)S(1)}, f32[38,128,128]{2,1,0:T(8,128)}, u32[]{:S(2)}) copy-start(f32[38,128,128]{2,1,0:T(8,128)} %param.10) | copy-start | bytes 7471108
  3.5 12.9 %collective-permute-start.2 = (f32[39,128,3]{1,0,2:T(8,128)S(1)}, f32[39,128,3]{1,0,2:T(8,128)}, u32[]{:S(2)}, u32[]{:S(2)}) collective-permute-start(f32[39,128,3]{1,0,2:T(8,128)S(1)} %get-tuple-element.18), channel_id=1, source_target_pairs={{0,1},{1,2},{2,3},{4,5},{5,6},{6,7},{8,9},{9,10},{10,11},{12,13},{... | collective-permute-start | bytes 179720 | tf_op jit(solution)/shard_map/ppermute | solution.py:25
  9.2 7.9 %collective-permute-start.3 = (f32[39,128,3]{1,0,2:T(8,128)S(1)}, f32[39,128,3]{1,0,2:T(8,128)}, u32[]{:S(2)}, u32[]{:S(2)}) collective-permute-start(f32[39,128,3]{1,0,2:T(8,128)S(1)} %get-tuple-element.19), channel_id=1, source_target_pairs={{1,0},{2,1},{3,2},{5,4},{6,5},{7,6},{9,8},{10,9},{11,10},{13,12},{... | collective-permute-start | bytes 179720 | tf_op jit(solution)/shard_map/ppermute | solution.py:25
  11.9 4.0 %copy-start.7 = (f32[128,128]{1,0:T(8,128)S(1)}, f32[128,128]{1,0:T(8,128)}, u32[]{:S(2)}) copy-start(f32[128,128]{1,0:T(8,128)} %param.12) | copy-start | bytes 196612
  11.9 4.1 %copy-start.11 = (s32[64,1]{0,1:T(1,128)S(1)}, s32[64,1]{0,1:T(1,128)}, u32[]{:S(2)}) copy-start(s32[64,1]{0,1:T(1,128)} %param.15) | copy-start | bytes 772
  12.6 5.2 %collective-permute-start = (f32[39,3,128]{2,0,1:T(8,128)}, f32[39,3,128]{2,0,1:T(8,128)}, u32[]{:S(2)}, u32[]{:S(2)}) collective-permute-start(f32[39,3,128]{2,0,1:T(8,128)} %get-tuple-element.16), channel_id=1, source_target_pairs={{0,4},{4,8},{8,12},{12,16},{16,20},{20,24},{24,28},{1,5},{5,9},{9,... | collective-permute-start | bytes 179720 | tf_op jit(solution)/shard_map/ppermute | solution.py:25
  14.7 4.4 %collective-permute-start.1 = (f32[39,3,128]{2,0,1:T(8,128)}, f32[39,3,128]{2,0,1:T(8,128)}, u32[]{:S(2)}, u32[]{:S(2)}) collective-permute-start(f32[39,3,128]{2,0,1:T(8,128)} %get-tuple-element.17), channel_id=1, source_target_pairs={{4,0},{8,4},{12,8},{16,12},{20,16},{24,20},{28,24},{5,1},{9,5},{13... | collective-permute-start | bytes 179720 | tf_op jit(solution)/shard_map/ppermute | solution.py:25
  26.3 9.6 %copy-start.1 = (f32[38,3,128]{1,0,2:T(8,128)S(1)}, f32[38,3,128]{1,0,2:T(8,128)}, u32[]{:S(2)}) copy-start(f32[38,3,128]{1,0,2:T(8,128)} %copy.123) | copy-start | bytes 175108
  26.3 9.6 %copy-start.2 = (f32[38,3,128]{1,0,2:T(8,128)S(1)}, f32[38,3,128]{1,0,2:T(8,128)}, u32[]{:S(2)}) copy-start(f32[38,3,128]{1,0,2:T(8,128)} %copy.126) | copy-start | bytes 175108
  51.2 1.0 %copy-start.4 = (f32[38,38]{1,0:T(8,128)S(1)}, f32[38,38]{1,0:T(8,128)}, u32[]{:S(2)}) copy-start(f32[38,38]{1,0:T(8,128)} %param.13) | copy-start | bytes 17332
  52.2 2.4 %copy-start.6 = (f32[38,38]{1,0:T(8,128)S(1)}, f32[38,38]{1,0:T(8,128)}, u32[]{:S(2)}) copy-start(f32[38,38]{1,0:T(8,128)} %param.14) | copy-start | bytes 17332
  68.0 4.4 %copy-start.9 = (f32[4,38]{1,0:T(4,128)S(1)}, f32[4,38]{1,0:T(4,128)}, u32[]{:S(2)}) copy-start(f32[4,38]{1,0:T(4,128)} %param.16) | copy-start | bytes 1828
  72.4 1.7 %copy-start.10 = (f32[128]{0:T(128)S(1)}, f32[128]{0:T(128)}, u32[]{:S(2)}) copy-start(f32[128]{0:T(128)} %param.17) | copy-start | bytes 1540
  74.3 4.2 %collective-permute-start.4 = (f32[4,128]{1,0:T(4,128)S(1)}, f32[4,128]{1,0:T(4,128)S(1)}, u32[]{:S(2)}, u32[]{:S(2)}) collective-permute-start(f32[4,128]{1,0:T(4,128)S(1)} %broadcast_multiply_fusion), channel_id=1, source_target_pairs={{0,1},{1,0},{2,3},{3,2},{4,5},{5,4},{6,7},{7,6},{8,9},{9,8},{10,11... | collective-permute-start | bytes 6152 | tf_op jit(solution)/shard_map/ppermute | solution.py:121
  78.6 4.5 %collective-permute-start.5 = (f32[4,128]{1,0:T(4,128)S(1)}, f32[4,128]{1,0:T(4,128)S(1)}, u32[]{:S(2)}, u32[]{:S(2)}) collective-permute-start(f32[4,128]{1,0:T(4,128)S(1)} %fusion.75), channel_id=1, source_target_pairs={{0,2},{1,3},{2,0},{3,1},{4,6},{5,7},{6,4},{7,5},{8,10},{9,11},{10,... | collective-permute-start | bytes 6152 | tf_op jit(solution)/shard_map/ppermute | solution.py:121
  83.1 1.7 %collective-permute-start.6 = (f32[1,4,128]{2,0,1:T(1,128)S(1)}, f32[1,4,128]{2,0,1:T(1,128)S(1)}, u32[]{:S(2)}, u32[]{:S(2)}) collective-permute-start(f32[1,4,128]{2,0,1:T(1,128)S(1)} %bitcast.98), channel_id=1, source_target_pairs={{0,4},{4,0},{8,12},{12,8},{16,20},{20,16},{24,28},{28,24},{1,5},{5... | collective-permute-start | bytes 6152 | tf_op jit(solution)/shard_map/ppermute | solution.py:134
  84.7 4.3 %collective-permute-start.7 = (f32[2,4,128]{2,0,1:T(2,128)S(1)}, f32[2,4,128]{2,0,1:T(2,128)S(1)}, u32[]{:S(2)}, u32[]{:S(2)}) collective-permute-start(f32[2,4,128]{2,0,1:T(2,128)S(1)} %maximum_select_fusion.2), channel_id=1, source_target_pairs={{0,8},{4,12},{8,0},{12,4},{16,24},{20,28},{24,16},{28,20},{1,9},{5... | collective-permute-start | bytes 12296 | tf_op jit(solution)/shard_map/ppermute | solution.py:134
  89.1 5.1 %collective-permute-start.8 = (f32[4,4,128]{2,0,1:T(4,128)S(1)}, f32[4,4,128]{2,0,1:T(4,128)S(1)}, u32[]{:S(2)}, u32[]{:S(2)}) collective-permute-start(f32[4,4,128]{2,0,1:T(4,128)S(1)} %maximum_select_fusion.1), channel_id=1, source_target_pairs={{0,16},{4,20},{8,24},{12,28},{16,0},{20,4},{24,8},{28,12},{1,17},{... | collective-permute-start | bytes 24584 | tf_op jit(solution)/shard_map/ppermute | solution.py:134
  92.1 5.0 %copy-start.8 = (f32[4,1024]{1,0:T(4,128)S(1)}, f32[4,1024]{1,0:T(4,128)}, u32[]{:S(2)}) copy-start(f32[4,1024]{1,0:T(4,128)} %param.19) | copy-start | bytes 49156
where the time goes:
time: 98.2 us; the launch traced here: 97.7 us
  other arithmetic  30.1 us (31%)
  starting transfers between devices  22.2 us (23%)
  matrix products  22 us (22%)
  local copies, waits for them, and re-layouts  16.1 us (16%)
  waiting for transfers between devices  6.39 us (7%)
  between operations  1.01 us (1%)
    mul x4, other arithmetic, face_difference(): face_flux = face_speed * weno_side(*stencil)  24.9 us
    dot_general x3, matrix products, kinetics_advance(): jnp.tensordot(frozen_jacobian_inverse_addend, defect, axes=(1, 0), precis...  12.9 us
    ppermute x4, starting transfers between devices, edge_layers(): return (lax.ppermute(last, axis, up), lax.ppermute(initial, axis, down))  10.3 us
    dot_general x3, matrix products, kinetics_advance(): jnp.tensordot(linearized_kinetics_operator, current, axes=(1, 0), precisi...  7.2 us
    ppermute x3, starting transfers between devices, doubling_gather(): other = lax.ppermute(blocks, axis, pairs)  6.61 us
    unnamed x33, local copies, waits for them, and re-layouts  6.4 us
    ppermute x2, starting transfers between devices, butterfly_sum(): part = part + lax.ppermute(part, axis, pairs)  5.28 us
    ppermute x2, waiting for transfers between devices, butterfly_sum(): part = part + lax.ppermute(part, axis, pairs)  3.45 us
  transfers between devices with their start and end apart: 9, of which 5 were waited for; matrix products, arithmetic and copies ran while one was open for 7% of the time, Pallas kernels for 0%

commit v1 on v0

--- a/solution.py
+++ b/solution.py
@@ -14,6 +14,7 @@
 ARRHENIUS_BARRIER = 1.0
 WENO_EPS = 1e-06
 HIGHEST = lax.Precision.HIGHEST
+CHEMISTRY_PRECISION = lax.Precision.HIGH
 
 
 def edge_layers(shard, axis, dim, width):
@@ -96,13 +97,13 @@
     current = starting_composition_field
     for newton_step in range(ITERS):
         source = jnp.tensordot(
-            linearized_kinetics_operator, current, axes=(1, 0), precision=HIGHEST
+            linearized_kinetics_operator, current, axes=(1, 0), precision=CHEMISTRY_PRECISION
         ) - jnp.tanh(current)
         defect = current - starting_composition_field - CHEM_STEP * acceleration_factor * source
         current = (
             current
             - defect
-            - jnp.tensordot(frozen_jacobian_inverse_addend, defect, axes=(1, 0), precision=HIGHEST)
+            - jnp.tensordot(frozen_jacobian_inverse_addend, defect, axes=(1, 0), precision=CHEMISTRY_PRECISION)
         )
     return current
 

time: 98.2 us -> 90.8 us (0.925)
  matrix products: 22 us -> 14.6 us
    dot_general x3, matrix products: 12.9 us -> 8.81 us  [kinetics_advance(): jnp.tensordot(frozen_jacobian_inverse_addend, defect, axes=(1, 0), precis...]
    dot_general x3, matrix products: 7.2 us -> 3.83 us  [kinetics_advance(): jnp.tensordot(linearized_kinetics_operator, current, axes=(1, 0), precisi...]
where the time goes in v1:
time: 90.8 us; the launch traced here: 90.3 us
  other arithmetic  30.1 us (33%)
  starting transfers between devices  22.2 us (24%)
  local copies, waits for them, and re-layouts  16.1 us (18%)
  matrix products  14.6 us (16%)
  waiting for transfers between devices  6.39 us (7%)
  between operations  1.02 us (1%)
    mul x4, other arithmetic, face_difference(): face_flux = face_speed * weno_side(*stencil)  24.9 us
    ppermute x4, starting transfers between devices, edge_layers(): return (lax.ppermute(last, axis, up), lax.ppermute(initial, axis, down))  10.3 us
    dot_general x3, matrix products, kinetics_advance(): jnp.tensordot(frozen_jacobian_inverse_addend, defect, axes=(1, 0), precis...  8.81 us
    ppermute x3, starting transfers between devices, doubling_gather(): other = lax.ppermute(blocks, axis, pairs)  6.61 us
    unnamed x33, local copies, waits for them, and re-layouts  6.4 us
    ppermute x2, starting transfers between devices, butterfly_sum(): part = part + lax.ppermute(part, axis, pairs)  5.28 us
    dot_general x3, matrix products, kinetics_advance(): jnp.tensordot(linearized_kinetics_operator, current, axes=(1, 0), precisi...  3.83 us
    ppermute x2, waiting for transfers between devices, butterfly_sum(): part = part + lax.ppermute(part, axis, pairs)  3.45 us
  transfers between devices with their start and end apart: 9, of which 5 were waited for; matrix products, arithmetic and copies ran while one was open for 7% of the time, Pallas kernels for 0%

profile of v1, /device:TPU:0, one launch (start us, length us, event | category | flops | bytes accessed | tf_op | source)
XLA Modules:
  0.0 90.3 jit_solution(11514641045696735457)
XLA Ops:
  0.7 2.6 %copy.134 = f32[38,128,128]{1,0,2:T(8,128)S(1)} copy(f32[38,128,128]{2,1,0:T(8,128)} %param.10) | data formatting | bytes 4980736 | tf_op args[0]
  3.5 5.7 %collective-permute-start.2 = (f32[39,128,3]{1,0,2:T(8,128)S(1)}, f32[39,128,3]{1,0,2:T(8,128)}, u32[]{:S(2)}, u32[]{:S(2)}) collective-permute-start(f32[39,128,3]{1,0,2:T(8,128)S(1)} %get-tuple-element.18), channel_id=1, source_target_pairs={{0,1},{1,2},{2,3},{4,5},{5,6},{6,7},{8,9},{9,10},{10,11},{12,13},{... | collective-permute-start | bytes 179720 | tf_op jit(solution)/shard_map/ppermute | solution.py:26
  9.2 1.3 %collective-permute-start.3 = (f32[39,128,3]{1,0,2:T(8,128)S(1)}, f32[39,128,3]{1,0,2:T(8,128)}, u32[]{:S(2)}, u32[]{:S(2)}) collective-permute-start(f32[39,128,3]{1,0,2:T(8,128)S(1)} %get-tuple-element.19), channel_id=1, source_target_pairs={{1,0},{2,1},{3,2},{5,4},{6,5},{7,6},{9,8},{10,9},{11,10},{13,12},{... | collective-permute-start | bytes 179720 | tf_op jit(solution)/shard_map/ppermute | solution.py:26
  10.5 1.5 %copy.117 = f32[38,128,128]{2,0,1:T(8,128)S(1)} copy(f32[38,128,128]{2,1,0:T(8,128)S(1)} %copy-done.3) | data formatting | bytes 4980736 | tf_op args[0]
  12.6 2.1 %collective-permute-start = (f32[39,3,128]{2,0,1:T(8,128)}, f32[39,3,128]{2,0,1:T(8,128)}, u32[]{:S(2)}, u32[]{:S(2)}) collective-permute-start(f32[39,3,128]{2,0,1:T(8,128)} %get-tuple-element.16), channel_id=1, source_target_pairs={{0,4},{4,8},{8,12},{12,16},{16,20},{20,24},{24,28},{1,5},{5,9},{9,... | collective-permute-start | bytes 179720 | tf_op jit(solution)/shard_map/ppermute | solution.py:26
  14.7 1.3 %collective-permute-start.1 = (f32[39,3,128]{2,0,1:T(8,128)}, f32[39,3,128]{2,0,1:T(8,128)}, u32[]{:S(2)}, u32[]{:S(2)}) collective-permute-start(f32[39,3,128]{2,0,1:T(8,128)} %get-tuple-element.17), channel_id=1, source_target_pairs={{4,0},{8,4},{12,8},{16,12},{20,16},{24,20},{28,24},{5,1},{9,5},{13... | collective-permute-start | bytes 179720 | tf_op jit(solution)/shard_map/ppermute | solution.py:26
  16.4 0.7 slice.176
  17.1 0.7 slice.177
  17.8 0.7 slice.162
  20.1 3.1 %copy.123 = f32[38,3,128]{1,0,2:T(8,128)} copy(f32[38,3,128]{2,0,1:T(8,128)} %bitcast.92) | data formatting | bytes 116736 | tf_op jit(solution)/shard_map/slice | solution.py:81
  23.2 3.1 %copy.126 = f32[38,3,128]{1,0,2:T(8,128)} copy(f32[38,3,128]{2,0,1:T(8,128)} %bitcast.91) | data formatting | bytes 116736 | tf_op jit(solution)/shard_map/slice | solution.py:81
  26.3 9.8 %divide_multiply_fusion.1 = f32[38,128,129]{1,0,2:T(8,128)S(1)} fusion(f32[38,128,3]{1,0,2:T(8,128)} %bitcast.89, f32[38,128,128]{1,0,2:T(8,128)S(1)} %copy.134, f32[38,128,3]{1,0,2:T(8,128)} %bitcast.90, f32[128,129]{0,1:T(8,128)S(1)} %fusion.62, pred[128,129]{0,1:T(8,128)(4,1)S(1)} %compare_bitcast_fusion), kind=kLoop, calls=%fused_computation.61 | loop fusion | flops 47686656 | bytes 5199488 | tf_op jit(solution)/shard_map/mul | solution.py:69
  36.1 15.1 %divide_multiply_fusion = f32[38,129,128]{1,0,2:T(8,128)S(1)} fusion(f32[38,3,128]{1,0,2:T(8,128)S(1)} %copy-done.2, f32[38,128,128]{1,0,2:T(8,128)S(1)} %copy.134, f32[38,3,128]{1,0,2:T(8,128)S(1)} %copy-done.1, f32[129,128]{0,1:T(8,128)S(1)} %copy.121, pred[129,128]{0,1:T(8,128)(4,1)S(1)} %copy.122), kind=kLoop, calls=%fused_computation.32 | loop fusion | flops 47686656 | bytes 5199488 | tf_op jit(solution)/shard_map/mul | solution.py:69
  51.2 1.0 %fusion.32 = f32[38,128,128]{1,0,2:T(8,128)S(1)} fusion(f32[38,128,128]{1,0,2:T(8,128)S(1)} %copy.134, f32[38,128,129]{1,0,2:T(8,128)S(1)} %divide_multiply_fusion.1, f32[38,129,128]{1,0,2:T(8,128)S(1)} %divide_multiply_fusion), kind=kLoop, calls=%fused_computation.67 | loop fusion | flops 3112960 | bytes 14942208 | tf_op jit(solution)/shard_map/sub | solution.py:87
  52.2 1.3 %fusion.70 = f32[128,128,38]{0,2,1:T(8,128)S(1)} fusion(f32[38,128,128]{1,0,2:T(8,128)S(1)} %fusion.32, f32[38,38]{1,0:T(8,128)S(1)} %copy-done.4), kind=kOutput, calls=%fused_computation.117 | convolution fusion | flops 141950976 | bytes 4986512 | tf_op jit(solution)/shard_map/dot_general | solution.py:99
  53.5 2.5 %bitcast_subtract_fusion.4 = f32[38,128,128]{1,0,2:T(8,128)S(1)} fusion(f32[38,128,128]{1,0,2:T(8,128)S(1)} %fusion.32, f32[128,128,38]{0,2,1:T(8,128)S(1)} %fusion.70, f32[128,128]{0,1:T(8,128)S(1)} %copy.135, f32[38,38]{1,0:T(8,128)S(1)} %copy-done.6), kind=kOutput, calls=%fused_computation.78 | convolution fusion | flops 148176896 | bytes 7542416 | tf_op jit(solution)/shard_map/dot_general | solution.py:106
  56.0 1.3 %fusion.68 = f32[128,128,38]{0,2,1:T(8,128)S(1)} fusion(f32[38,128,128]{1,0,2:T(8,128)S(1)} %bitcast_subtract_fusion.4, f32[38,38]{1,0:T(8,128)S(1)} %copy-done.4), kind=kOutput, calls=%fused_computation.115 | convolution fusion | flops 141950976 | bytes 4986512 | tf_op jit(solution)/shard_map/dot_general | solution.py:99
  57.3 3.0 %bitcast_subtract_fusion.2 = f32[38,128,128]{1,0,2:T(8,128)S(1)} fusion(f32[38,128,128]{1,0,2:T(8,128)S(1)} %bitcast_subtract_fusion.4, f32[128,128,38]{0,2,1:T(8,128)S(1)} %fusion.68, f32[38,128,128]{1,0,2:T(8,128)S(1)} %fusion.32, f32[128,128]{0,1:T(8,128)S(1)} %copy.135, f32[38,38]{1,0:T(8,128)S(1)} %copy-done.6), kind=kOutput, calls=%fused_computation.74 | convolution fusion | flops 148176896 | bytes 10032784 | tf_op jit(solution)/shard_map/dot_general | solution.py:106
  60.3 1.3 %fusion.66 = f32[128,128,38]{0,2,1:T(8,128)S(1)} fusion(f32[38,128,128]{1,0,2:T(8,128)S(1)} %bitcast_subtract_fusion.2, f32[38,38]{1,0:T(8,128)S(1)} %copy-done.4), kind=kOutput, calls=%fused_computation.113 | convolution fusion | flops 141950976 | bytes 4986512 | tf_op jit(solution)/shard_map/dot_general | solution.py:99
  61.6 3.3 %fusion.33 = f32[38,128,128]{1,0,2:T(8,128)S(1)} fusion(f32[38,128,128]{1,0,2:T(8,128)S(1)} %fusion.32, f32[38,128,128]{1,0,2:T(8,128)S(1)} %bitcast_subtract_fusion.2, f32[128,128,38]{0,2,1:T(8,128)S(1)} %fusion.66, f32[128,128]{0,1:T(8,128)S(1)} %copy.135, pred[128]{0:T(512)(128)(4,1)S(1)} %gt.22, f32[38,38]{1,0:T(8,128)S(1)} %copy-done.6), kind=kOutput, calls=%fused_computation.70 | convolution fusion | flops 148799488 | bytes 10032912 | tf_op jit(solution)/shard_map/dot_general | solution.py:106
  65.0 1.7 %convolution_bitcast_fusion = f32[4,128,128]{1,0,2:T(4,128)S(1)} fusion(f32[38,128,128]{1,0,2:T(8,128)S(1)} %fusion.33, f32[4,38]{1,0:T(4,128)S(1)} %copy-done.9), kind=kOutput, calls=%fused_computation.90 | convolution fusion | flops 29884416 | bytes 2753120 | tf_op jit(solution)/shard_map/dot_general | solution.py:112
  66.9 2.7 %collective-permute-start.4 = (f32[4,128]{1,0:T(4,128)S(1)}, f32[4,128]{1,0:T(4,128)S(1)}, u32[]{:S(2)}, u32[]{:S(2)}) collective-permute-start(f32[4,128]{1,0:T(4,128)S(1)} %broadcast_multiply_fusion), channel_id=1, source_target_pairs={{0,1},{1,0},{2,3},{3,2},{4,5},{5,4},{6,7},{7,6},{8,9},{9,8},{10,11... | collective-permute-start | bytes 6152 | tf_op jit(solution)/shard_map/ppermute | solution.py:122
  69.6 1.6 %collective-permute-done.4 = f32[4,128]{1,0:T(4,128)S(1)} collective-permute-done((f32[4,128]{1,0:T(4,128)S(1)}, f32[4,128]{1,0:T(4,128)S(1)}, u32[]{:S(2)}, u32[]{:S(2)}) %collective-permute-start.4) | collective-permute-done | bytes 2080 | tf_op jit(solution)/shard_map/ppermute | solution.py:122
  71.1 2.6 %collective-permute-start.5 = (f32[4,128]{1,0:T(4,128)S(1)}, f32[4,128]{1,0:T(4,128)S(1)}, u32[]{:S(2)}, u32[]{:S(2)}) collective-permute-start(f32[4,128]{1,0:T(4,128)S(1)} %fusion.75), channel_id=1, source_target_pairs={{0,2},{1,3},{2,0},{3,1},{4,6},{5,7},{6,4},{7,5},{8,10},{9,11},{10,... | collective-permute-start | bytes 6152 | tf_op jit(solution)/shard_map/ppermute | solution.py:122
  73.7 1.9 %collective-permute-done.5 = f32[4,128]{1,0:T(4,128)S(1)} collective-permute-done((f32[4,128]{1,0:T(4,128)S(1)}, f32[4,128]{1,0:T(4,128)S(1)}, u32[]{:S(2)}, u32[]{:S(2)}) %collective-permute-start.5) | collective-permute-done | bytes 2080 | tf_op jit(solution)/shard_map/ppermute | solution.py:122
  75.6 0.9 collective-permute-start.6
  76.5 0.8 collective-permute-done.6
  77.3 2.7 %collective-permute-start.7 = (f32[2,4,128]{2,0,1:T(2,128)S(1)}, f32[2,4,128]{2,0,1:T(2,128)S(1)}, u32[]{:S(2)}, u32[]{:S(2)}) collective-permute-start(f32[2,4,128]{2,0,1:T(2,128)S(1)} %maximum_select_fusion.2), channel_id=1, source_target_pairs={{0,8},{4,12},{8,0},{12,4},{16,24},{20,28},{24,16},{28,20},{1,9},{5... | collective-permute-start | bytes 12296 | tf_op jit(solution)/shard_map/ppermute | solution.py:135
  80.1 1.6 %collective-permute-done.7 = f32[2,4,128]{2,0,1:T(2,128)S(1)} collective-permute-done((f32[2,4,128]{2,0,1:T(2,128)S(1)}, f32[2,4,128]{2,0,1:T(2,128)S(1)}, u32[]{:S(2)}, u32[]{:S(2)}) %collective-permute-start.7) | collective-permute-done | bytes 4128 | tf_op jit(solution)/shard_map/ppermute | solution.py:135
  81.7 3.0 %collective-permute-start.8 = (f32[4,4,128]{2,0,1:T(4,128)S(1)}, f32[4,4,128]{2,0,1:T(4,128)S(1)}, u32[]{:S(2)}, u32[]{:S(2)}) collective-permute-start(f32[4,4,128]{2,0,1:T(4,128)S(1)} %maximum_select_fusion.1), channel_id=1, source_target_pairs={{0,16},{4,20},{8,24},{12,28},{16,0},{20,4},{24,8},{28,12},{1,17},{... | collective-permute-start | bytes 24584 | tf_op jit(solution)/shard_map/ppermute | solution.py:135
  84.7 2.1 %copy.136 = f32[38,128,128]{2,1,0:T(8,128)} copy(f32[38,128,128]{1,0,2:T(8,128)S(1)} %fusion.33) | data formatting | bytes 4980736
  86.8 2.8 %select_reduce_fusion = f32[4,1024]{1,0:T(4,128)S(1)} fusion(f32[4,1024]{1,0:T(4,128)S(1)} %bitcast.95, s32[4,1024]{1,0:T(4,128)S(1)} %constant_dynamic-slice_fusion), kind=kLoop, calls=%fused_computation | loop fusion | flops 12578816 | bytes 49152 | tf_op jit(solution)/shard_map/reduce_sum | solution.py:187
  (59 shorter events, 3.7 us)
Async XLA Ops:
  0.6 84.1 %copy-start = (s32[4,32768]{1,0:T(4,128)S(1)}, s32[4,32768]{1,0:T(4,128)}, u32[]{:S(2)}) copy-start(s32[4,32768]{1,0:T(4,128)} %param.18) | copy-start | bytes 1572868
  0.6 2.7 %copy-start.5 = (f32[2,128,128]{2,1,0:T(8,128)S(1)}, f32[2,128,128]{2,1,0:T(8,128)}, u32[]{:S(2)}) copy-start(f32[2,128,128]{2,1,0:T(8,128)} %param.11) | copy-start | bytes 393220
  3.4 7.0 %copy-start.3 = (f32[38,128,128]{2,1,0:T(8,128)S(1)}, f32[38,128,128]{2,1,0:T(8,128)}, u32[]{:S(2)}) copy-start(f32[38,128,128]{2,1,0:T(8,128)} %param.10) | copy-start | bytes 7471108
  3.5 12.9 %collective-permute-start.2 = (f32[39,128,3]{1,0,2:T(8,128)S(1)}, f32[39,128,3]{1,0,2:T(8,128)}, u32[]{:S(2)}, u32[]{:S(2)}) collective-permute-start(f32[39,128,3]{1,0,2:T(8,128)S(1)} %get-tuple-element.18), channel_id=1, source_target_pairs={{0,1},{1,2},{2,3},{4,5},{5,6},{6,7},{8,9},{9,10},{10,11},{12,13},{... | collective-permute-start | bytes 179720 | tf_op jit(solution)/shard_map/ppermute | solution.py:26
  9.2 7.9 %collective-permute-start.3 = (f32[39,128,3]{1,0,2:T(8,128)S(1)}, f32[39,128,3]{1,0,2:T(8,128)}, u32[]{:S(2)}, u32[]{:S(2)}) collective-permute-start(f32[39,128,3]{1,0,2:T(8,128)S(1)} %get-tuple-element.19), channel_id=1, source_target_pairs={{1,0},{2,1},{3,2},{5,4},{6,5},{7,6},{9,8},{10,9},{11,10},{13,12},{... | collective-permute-start | bytes 179720 | tf_op jit(solution)/shard_map/ppermute | solution.py:26
  11.9 4.0 %copy-start.7 = (f32[128,128]{1,0:T(8,128)S(1)}, f32[128,128]{1,0:T(8,128)}, u32[]{:S(2)}) copy-start(f32[128,128]{1,0:T(8,128)} %param.12) | copy-start | bytes 196612
  11.9 4.1 %copy-start.11 = (s32[64,1]{0,1:T(1,128)S(1)}, s32[64,1]{0,1:T(1,128)}, u32[]{:S(2)}) copy-start(s32[64,1]{0,1:T(1,128)} %param.15) | copy-start | bytes 772
  12.6 5.2 %collective-permute-start = (f32[39,3,128]{2,0,1:T(8,128)}, f32[39,3,128]{2,0,1:T(8,128)}, u32[]{:S(2)}, u32[]{:S(2)}) collective-permute-start(f32[39,3,128]{2,0,1:T(8,128)} %get-tuple-element.16), channel_id=1, source_target_pairs={{0,4},{4,8},{8,12},{12,16},{16,20},{20,24},{24,28},{1,5},{5,9},{9,... | collective-permute-start | bytes 179720 | tf_op jit(solution)/shard_map/ppermute | solution.py:26
  14.7 4.4 %collective-permute-start.1 = (f32[39,3,128]{2,0,1:T(8,128)}, f32[39,3,128]{2,0,1:T(8,128)}, u32[]{:S(2)}, u32[]{:S(2)}) collective-permute-start(f32[39,3,128]{2,0,1:T(8,128)} %get-tuple-element.17), channel_id=1, source_target_pairs={{4,0},{8,4},{12,8},{16,12},{20,16},{24,20},{28,24},{5,1},{9,5},{13... | collective-permute-start | bytes 179720 | tf_op jit(solution)/shard_map/ppermute | solution.py:26
  26.3 9.8 %copy-start.1 = (f32[38,3,128]{1,0,2:T(8,128)S(1)}, f32[38,3,128]{1,0,2:T(8,128)}, u32[]{:S(2)}) copy-start(f32[38,3,128]{1,0,2:T(8,128)} %copy.123) | copy-start | bytes 175108
  26.3 9.8 %copy-start.2 = (f32[38,3,128]{1,0,2:T(8,128)S(1)}, f32[38,3,128]{1,0,2:T(8,128)}, u32[]{:S(2)}) copy-start(f32[38,3,128]{1,0,2:T(8,128)} %copy.126) | copy-start | bytes 175108
  51.2 1.0 %copy-start.4 = (f32[38,38]{1,0:T(8,128)S(1)}, f32[38,38]{1,0:T(8,128)}, u32[]{:S(2)}) copy-start(f32[38,38]{1,0:T(8,128)} %param.13) | copy-start | bytes 17332
  52.2 1.3 %copy-start.6 = (f32[38,38]{1,0:T(8,128)S(1)}, f32[38,38]{1,0:T(8,128)}, u32[]{:S(2)}) copy-start(f32[38,38]{1,0:T(8,128)} %param.14) | copy-start | bytes 17332
  61.6 3.3 %copy-start.9 = (f32[4,38]{1,0:T(4,128)S(1)}, f32[4,38]{1,0:T(4,128)}, u32[]{:S(2)}) copy-start(f32[4,38]{1,0:T(4,128)} %param.16) | copy-start | bytes 1828
  65.0 1.7 %copy-start.10 = (f32[128]{0:T(128)S(1)}, f32[128]{0:T(128)}, u32[]{:S(2)}) copy-start(f32[128]{0:T(128)} %param.17) | copy-start | bytes 1540
  66.9 4.2 %collective-permute-start.4 = (f32[4,128]{1,0:T(4,128)S(1)}, f32[4,128]{1,0:T(4,128)S(1)}, u32[]{:S(2)}, u32[]{:S(2)}) collective-permute-start(f32[4,128]{1,0:T(4,128)S(1)} %broadcast_multiply_fusion), channel_id=1, source_target_pairs={{0,1},{1,0},{2,3},{3,2},{4,5},{5,4},{6,7},{7,6},{8,9},{9,8},{10,11... | collective-permute-start | bytes 6152 | tf_op jit(solution)/shard_map/ppermute | solution.py:122
  71.1 4.5 %collective-permute-start.5 = (f32[4,128]{1,0:T(4,128)S(1)}, f32[4,128]{1,0:T(4,128)S(1)}, u32[]{:S(2)}, u32[]{:S(2)}) collective-permute-start(f32[4,128]{1,0:T(4,128)S(1)} %fusion.75), channel_id=1, source_target_pairs={{0,2},{1,3},{2,0},{3,1},{4,6},{5,7},{6,4},{7,5},{8,10},{9,11},{10,... | collective-permute-start | bytes 6152 | tf_op jit(solution)/shard_map/ppermute | solution.py:122
  75.6 1.7 %collective-permute-start.6 = (f32[1,4,128]{2,0,1:T(1,128)S(1)}, f32[1,4,128]{2,0,1:T(1,128)S(1)}, u32[]{:S(2)}, u32[]{:S(2)}) collective-permute-start(f32[1,4,128]{2,0,1:T(1,128)S(1)} %bitcast.98), channel_id=1, source_target_pairs={{0,4},{4,0},{8,12},{12,8},{16,20},{20,16},{24,28},{28,24},{1,5},{5... | collective-permute-start | bytes 6152 | tf_op jit(solution)/shard_map/ppermute | solution.py:135
  77.3 4.3 %collective-permute-start.7 = (f32[2,4,128]{2,0,1:T(2,128)S(1)}, f32[2,4,128]{2,0,1:T(2,128)S(1)}, u32[]{:S(2)}, u32[]{:S(2)}) collective-permute-start(f32[2,4,128]{2,0,1:T(2,128)S(1)} %maximum_select_fusion.2), channel_id=1, source_target_pairs={{0,8},{4,12},{8,0},{12,4},{16,24},{20,28},{24,16},{28,20},{1,9},{5... | collective-permute-start | bytes 12296 | tf_op jit(solution)/shard_map/ppermute | solution.py:135
  81.7 5.1 %collective-permute-start.8 = (f32[4,4,128]{2,0,1:T(4,128)S(1)}, f32[4,4,128]{2,0,1:T(4,128)S(1)}, u32[]{:S(2)}, u32[]{:S(2)}) collective-permute-start(f32[4,4,128]{2,0,1:T(4,128)S(1)} %maximum_select_fusion.1), channel_id=1, source_target_pairs={{0,16},{4,20},{8,24},{12,28},{16,0},{20,4},{24,8},{28,12},{1,17},{... | collective-permute-start | bytes 24584 | tf_op jit(solution)/shard_map/ppermute | solution.py:135
  84.7 5.0 %copy-start.8 = (f32[4,1024]{1,0:T(4,128)S(1)}, f32[4,1024]{1,0:T(4,128)}, u32[]{:S(2)}) copy-start(f32[4,1024]{1,0:T(4,128)} %param.19) | copy-start | bytes 49156
